TPU v7x, 512 devices: a whole 4x8x8 slice. The times are simulated.
512 devices in a mesh: gx: 32 (over z, y_hi, core), gy: 16 (over x, y_lo).
Axes of the slice: x: 4, y: 8 (y_hi: 2, y_lo: 4; y = y_hi * 4 + y_lo), z: 8, core: 2. Of those that a mesh axis runs over, the one named last changes fastest.
Arguments:
- design: float32 [256, 128, 128], P('gx', 'gy'), may hold values from 0.06 to 0.9
- passive: int32 [256, 128, 128], P('gx', 'gy'), may hold values 0 or 1
- basis_pairs: float32 [4, 2, 3, 256, 128, 128], P(None, None, None, 'gx', 'gy'), may hold values from -6 to 6
- supports: int32 [256, 128, 128], P('gx', 'gy'), may hold values 0 or 1
- stiffness: float32 [24, 24], replicated, may hold values from -1.25 to 1.25
- mass_matrix: float32 [24, 24], replicated, may hold values from -1.25 to 1.25
- volume_fraction: float32 [64], replicated, may hold values from 0.26 to 0.36
Outputs:
- sensitivity: float32 [256, 128, 128], P('gx', 'gy')
- design_next: float32 [256, 128, 128], P('gx', 'gy')
All inputs are finite; a program needn't handle non-finite values. No bound on the sum of `passive` or of `supports` on one device may be relied on, other than what follows from the above.
Results may differ from a plain program's by a relative error of at most 0.0003.
Values sent between devices are 32-bit elements; how exact they have to be, the bound alone decides.
No kernel may reach another device: no remote copies, remote signals or barrier semaphores. Data moves between devices by JAX's collectives and lax.ppermute only.
A program may use at most 64 MiB of HBM per device.

v0:
```python
import math
import jax
import jax.numpy as jnp
from jax import lax
from jax.sharding import PartitionSpec as P

BISECT = 6
REGIONS = 64
PENALTY_SCALE = 3.0 * (1.0 - 0.001)
OMEGA_SQUARED = 0.5
MOVE_LIMIT = 0.2


def with_halo(cells, sides, width):
    for axis, dim in sides:
        count = lax.axis_size(axis)
        ends = count - 1
        head = lax.slice_in_dim(cells, 0, width, axis=dim)
        tail = lax.slice_in_dim(cells, cells.shape[dim] - width, cells.shape[dim], axis=dim)
        cells = jnp.concatenate(
            [
                lax.ppermute(tail, axis, [(i, (i + 1) % count) for i in range(ends)]),
                cells,
                lax.ppermute(head, axis, [((i + 1) % count, i) for i in range(ends)]),
            ],
            axis=dim,
        )
    return cells


def from_behind(value, axis, steps):
    count = lax.axis_size(axis)
    initial, last = (max(0, -steps), min(count, count - steps))
    return lax.ppermute(value, axis, [(source, source + steps) for source in range(initial, last)])


def filter_taps():
    tap_list = []
    for offset_x in range(-2, 3):
        for offset_y in range(-2, 3):
            for offset_z in range(-2, 3):
                weight = 3.0 - math.sqrt(
                    offset_x * offset_x + offset_y * offset_y + offset_z * offset_z
                )
                if weight > 0.0:
                    tap_list.append((offset_x, offset_y, offset_z, weight))
    return tap_list


def stencil(padded, block_shape):
    result = jnp.zeros(block_shape, jnp.float32)
    for offset_x, offset_y, offset_z, weight in filter_taps():
        result = (
            result
            + weight
            * padded[
                2 + offset_x : 2 + offset_x + block_shape[0],
                2 + offset_y : 2 + offset_y + block_shape[1],
                2 + offset_z : 2 + offset_z + block_shape[2],
            ]
        )
    return result


def element_terms(extended, stiffness, mass_matrix):
    pair_count = extended.shape[0]
    cells_x = extended.shape[3] - 1
    cells_y = extended.shape[4] - 1
    cells_z = extended.shape[5] - 1
    stiff_energy = jnp.zeros((cells_x * cells_y * cells_z,), jnp.float32)
    mass_energy = jnp.zeros((cells_x * cells_y * cells_z,), jnp.float32)
    for pair_index in range(pair_count):
        vectors = []
        for member in range(2):
            row_list = []
            for corner_x in (0, 1):
                for corner_y in (0, 1):
                    for corner_z in (0, 1):
                        for component in range(3):
                            row_list.append(
                                extended[
                                    pair_index,
                                    member,
                                    component,
                                    corner_x : corner_x + cells_x,
                                    corner_y : corner_y + cells_y,
                                    corner_z : corner_z + cells_z,
                                ].reshape(-1)
                            )
            vectors.append(jnp.stack(row_list))
        state_rows, adjoint_rows = vectors
        stiff_energy = stiff_energy + jnp.sum(
            state_rows * jnp.dot(stiffness, adjoint_rows, precision=lax.Precision.HIGHEST), axis=0
        )
        mass_energy = mass_energy + jnp.sum(
            state_rows * jnp.dot(mass_matrix, adjoint_rows, precision=lax.Precision.HIGHEST), axis=0
        )
    return (
        stiff_energy.reshape(cells_x, cells_y, cells_z),
        mass_energy.reshape(cells_x, cells_y, cells_z),
    )


def shards(design, passive, basis_pairs, supports, stiffness, mass_matrix, volume_fraction):
    block_shape = design.shape
    size_x, size_y, size_z = block_shape
    devices_x = lax.axis_size("gx")
    devices_y = lax.axis_size("gy")
    index_x = lax.axis_index("gx")
    index_y = lax.axis_index("gy")
    grid_x = size_x * devices_x
    grid_y = size_y * devices_y
    spread_x = jnp.arange(size_x + 4, dtype=jnp.int32) + index_x * size_x - 2
    spread_y = jnp.arange(size_y + 4, dtype=jnp.int32) + index_y * size_y - 2
    valid_x = ((spread_x >= 0) & (spread_x < grid_x)).astype(jnp.float32)
    valid_y = ((spread_y >= 0) & (spread_y < grid_y)).astype(jnp.float32)
    valid_z = jnp.pad(jnp.ones((size_z,), jnp.float32), 2)
    inside = valid_x[:, None, None] * valid_y[None, :, None] * valid_z[None, None, :]
    weight_sum = stencil(inside, block_shape)
    design_wide = with_halo(design, (("gx", 0), ("gy", 1)), 2)
    design_wide = jnp.pad(design_wide, ((0, 0), (0, 0), (2, 2)))
    physical = jnp.where(passive == 1, 1.0, stencil(design_wide, block_shape) / weight_sum)
    fields = basis_pairs * (1 - supports).astype(jnp.float32)
    rim_first = from_behind(fields[:, :, :, :1], "gx", -1)
    widened = jnp.concatenate([fields, rim_first], axis=3)
    rim_second = from_behind(widened[:, :, :, :, :1], "gy", -1)
    extended = jnp.concatenate([widened, rim_second], axis=4)
    extended = jnp.pad(extended, ((0, 0), (0, 0), (0, 0), (0, 0), (0, 0), (0, 1)))
    stiff_energy, mass_energy = element_terms(extended, stiffness, mass_matrix)
    raw_sensitivity = -(
        PENALTY_SCALE * physical * physical * stiff_energy - OMEGA_SQUARED * mass_energy
    )
    raw_sensitivity = jnp.where(passive == 1, 0.0, raw_sensitivity)
    scaled_wide = with_halo(raw_sensitivity / weight_sum, (("gx", 0), ("gy", 1)), 2)
    scaled_wide = jnp.pad(scaled_wide, ((0, 0), (0, 0), (2, 2)))
    sensitivity = stencil(scaled_wide, block_shape)
    benefit = jnp.maximum(-sensitivity, 0.0)
    floor_value = jnp.maximum(design - MOVE_LIMIT, 0.0)
    ceiling = jnp.minimum(design + MOVE_LIMIT, 1.0)
    band_cells = size_z // REGIONS
    target = volume_fraction * float(grid_x * grid_y * band_cells)

    def candidate(multiplier):
        per_cell = jnp.repeat(multiplier, band_cells)[None, None, :]
        trial = design * jnp.sqrt(benefit / per_cell)
        return jnp.where(passive == 1, 1.0, jnp.minimum(ceiling, jnp.maximum(floor_value, trial)))

    def region_sum(field):
        return jnp.sum(field, axis=(0, 1)).reshape(REGIONS, band_cells).sum(axis=1)

    levels = BISECT

    def bisect_round(round_index, bracket):
        low_end, high_end = bracket
        level_nodes = [(low_end, high_end)]
        midpoints = []
        for depth in range(levels):
            next_nodes = []
            for node_low, node_high in level_nodes:
                middle = jnp.sqrt(node_low * node_high)
                midpoints.append(middle)
                next_nodes.append((node_low, middle))
                next_nodes.append((middle, node_high))
            level_nodes = next_nodes
        trial_multipliers = jnp.stack(midpoints)
        per_cell = jnp.repeat(trial_multipliers, band_cells, axis=1)[:, None, None, :]
        trial = design[None] * jnp.sqrt(benefit[None] / per_cell)
        fields_of = jnp.where(
            passive[None] == 1,
            1.0,
            jnp.minimum(ceiling[None], jnp.maximum(floor_value[None], trial)),
        )
        partial_volumes = (
            jnp.sum(fields_of, axis=(1, 2)).reshape(len(midpoints), REGIONS, band_cells).sum(axis=2)
        )
        volumes = lax.psum(partial_volumes, ("gx", "gy"))
        position = jnp.zeros((REGIONS,), jnp.int32)
        for depth in range(levels):
            middle = jnp.sqrt(low_end * high_end)
            heap_index = position + (2**depth - 1)
            chosen = jnp.take_along_axis(volumes, heap_index[None, :], axis=0)[0]
            heavier = chosen > target
            low_end = jnp.where(heavier, middle, low_end)
            high_end = jnp.where(heavier, high_end, middle)
            position = 2 * position + heavier.astype(jnp.int32)
        return (low_end, high_end)

    start = (jnp.full((REGIONS,), 0.0001, jnp.float32), jnp.full((REGIONS,), 10000.0, jnp.float32))
    low_end, high_end = bisect_round(0, start)
    design_next = candidate(jnp.sqrt(low_end * high_end))
    return (sensitivity, design_next)


def solution(mesh):
    placed = (
        P("gx", "gy", None),
        P("gx", "gy", None),
        P(None, None, None, "gx", "gy", None),
        P("gx", "gy", None),
        P(),
        P(),
        P(),
    )
    return jax.shard_map(
        shards,
        mesh=mesh,
        in_specs=placed,
        out_specs=(P("gx", "gy", None), P("gx", "gy", None)),
        check_vma=False,
    )
```

profile of v0, /device:TPU:1, one launch (start us, length us, event | category | flops | bytes accessed | tf_op | source)
XLA Modules:
  0.0 233.9 jit_solution(4660837941216454200)
XLA Ops:
  1.4 8.8 %collective-permute-start.1 = (f32[2,8,128]{2,1,0:T(8,128)S(1)}, f32[2,8,128]{2,1,0:T(8,128)S(1)}, u32[]{:S(2)}, u32[]{:S(2)}) collective-permute-start(f32[2,8,128]{2,1,0:T(8,128)S(1)} %get-tuple-element.214), channel_id=1, source_target_pairs={{16,0},{32,16},{48,32},{64,48},{80,64},{96,80},{112,96},{128,112},... | collective-permute-start | bytes 24584 | tf_op jit(solution)/shard_map/ppermute | solution.py:24
  10.2 2.0 collective-permute-start
  14.2 2.3 %collective-permute-start.4 = (f32[4,2,3,1,8,128]{5,4,3,2,1,0:T(8,128)S(1)}, f32[4,2,3,1,8,128]{5,4,3,2,1,0:T(8,128)S(1)}, u32[]{:S(2)}, u32[]{:S(2)}) collective-permute-start(f32[4,2,3,1,8,128]{5,4,3,2,1,0:T(8,128)S(1)} %slice.2424), channel_id=1, source_target_pairs={{16,0},{32,16},{48,32},{64,48},{80,64},{96,80},{112,96},{128,112},... | collective-permute-start | bytes 294920 | tf_op jit(solution)/shard_map/ppermute | solution.py:34
  18.3 2.3 collective-permute-start.2
  20.6 1.3 collective-permute-start.3
  22.4 2.7 %collective-permute-done.3 = f32[12,2,128]{2,1,0:T(2,128)S(1)} collective-permute-done((f32[12,2,128]{2,1,0:T(2,128)S(1)}, f32[12,2,128]{2,1,0:T(2,128)S(1)}, u32[]{:S(2)}, u32[]{:S(2)}) %collective-permute-start.3) | collective-permute-done | bytes 12320 | tf_op jit(solution)/shard_map/ppermute | solution.py:24
  29.0 4.9 %collective-permute-done.5 = f32[4,2,3,9,1,128]{5,3,4,2,1,0:T(8,128)S(1)} collective-permute-done((f32[4,2,3,9,1,128]{5,3,4,2,1,0:T(8,128)S(1)}, f32[4,2,3,9,1,128]{5,3,4,2,1,0:T(8,128)S(1)}, u32[]{:S(2)}, u32[]{:S(2)}) %collective-permute-start.5) | collective-permute-done | bytes 110624 | tf_op jit(solution)/shard_map/ppermute | solution.py:34
  40.0 3.7 %stack.24 = f32[24,8192]{1,0:T(8,128)S(1)} concatenate(f32[1,8192]{1,0:T(1,128)} %bitcast.576, f32[1,8192]{1,0:T(1,128)} %bitcast.575, f32[1,8192]{1,0:T(1,128)} %bitcast.574, f32[1,8192]{1,0:T(1,128)} %bitcast.624, f32[1,8192]{1,0:T(1,128)} %bitcast.497, f32[1,8192]{1,0:T(1,128)} %bitcast.498, f32[1,8192]{1,0:T(1,128)} %bitcast.623, f32[1,8192]{1,0:T(1,128)} %bitcast.622, ...), dimensions={0} | concatenate | bytes 1572864 | tf_op jit(solution)/shard_map/stack | solution.py:90
  43.8 5.8 %stack.25 = f32[24,8192]{1,0:T(8,128)} concatenate(f32[1,8192]{1,0:T(1,128)} %bitcast.571, f32[1,8192]{1,0:T(1,128)} %bitcast.570, f32[1,8192]{1,0:T(1,128)} %bitcast.588, f32[1,8192]{1,0:T(1,128)} %bitcast.468, f32[1,8192]{1,0:T(1,128)} %bitcast.469, f32[1,8192]{1,0:T(1,128)} %bitcast.470, f32[1,8192]{1,0:T(1,128)} %bitcast.617, f32[1,8192]{1,0:T(1,128)} %bitcast.616, ...), dimensions={0} | concatenate | bytes 1572864 | tf_op jit(solution)/shard_map/stack | solution.py:90
  49.6 2.7 %fusion.17 = f32[8192]{0:T(1024)} fusion(f32[24,8192]{1,0:T(8,128)S(1)} %stack.24, f32[24,8192]{1,0:T(8,128)} %stack.25, f32[24,24]{1,0:T(8,128)S(1)} %copy-done), kind=kOutput, calls=%fused_computation.153 | convolution fusion | flops 57008128 | bytes 1607936 | tf_op jit(solution)/shard_map/dot_general | solution.py:96
  52.3 1.5 fusion.13
  53.8 3.7 %stack.31 = f32[24,8192]{1,0:T(8,128)S(1)} concatenate(f32[1,8192]{1,0:T(1,128)} %bitcast.564, f32[1,8192]{1,0:T(1,128)} %bitcast.584, f32[1,8192]{1,0:T(1,128)} %bitcast.580, f32[1,8192]{1,0:T(1,128)} %bitcast.514, f32[1,8192]{1,0:T(1,128)} %bitcast.515, f32[1,8192]{1,0:T(1,128)} %bitcast.516, f32[1,8192]{1,0:T(1,128)} %bitcast.531, f32[1,8192]{1,0:T(1,128)} %bitcast.530, ...), dimensions={0} | concatenate | bytes 1572864 | tf_op jit(solution)/shard_map/stack | solution.py:90
  57.5 5.8 %stack.30 = f32[24,8192]{1,0:T(8,128)} concatenate(f32[1,8192]{1,0:T(1,128)} %bitcast.558, f32[1,8192]{1,0:T(1,128)} %bitcast.557, f32[1,8192]{1,0:T(1,128)} %bitcast.556, f32[1,8192]{1,0:T(1,128)} %bitcast.466, f32[1,8192]{1,0:T(1,128)} %bitcast.479, f32[1,8192]{1,0:T(1,128)} %bitcast.480, f32[1,8192]{1,0:T(1,128)} %bitcast.513, f32[1,8192]{1,0:T(1,128)} %bitcast.512, ...), dimensions={0} | concatenate | bytes 1572864 | tf_op jit(solution)/shard_map/stack | solution.py:90
  63.3 2.7 %fusion.20 = f32[8192]{0:T(1024)} fusion(f32[24,8192]{1,0:T(8,128)} %stack.30, f32[24,8192]{1,0:T(8,128)S(1)} %stack.31, f32[24,24]{1,0:T(8,128)S(1)} %copy-done), kind=kOutput, calls=%fused_computation.156 | convolution fusion | flops 57008128 | bytes 1607936 | tf_op jit(solution)/shard_map/dot_general | solution.py:96
  66.0 1.5 fusion.16
  69.5 3.7 %stack.27 = f32[24,8192]{1,0:T(8,128)S(1)} concatenate(f32[1,8192]{1,0:T(1,128)} %bitcast.569, f32[1,8192]{1,0:T(1,128)} %bitcast.568, f32[1,8192]{1,0:T(1,128)} %bitcast.567, f32[1,8192]{1,0:T(1,128)} %bitcast.534, f32[1,8192]{1,0:T(1,128)} %bitcast.535, f32[1,8192]{1,0:T(1,128)} %bitcast.536, f32[1,8192]{1,0:T(1,128)} %bitcast.610, f32[1,8192]{1,0:T(1,128)} %bitcast.609, ...), dimensions={0} | concatenate | bytes 1572864 | tf_op jit(solution)/shard_map/stack | solution.py:90
  73.3 3.6 %stack.26 = f32[24,8192]{1,0:T(8,128)S(1)} concatenate(f32[1,8192]{1,0:T(1,128)S(1)} %bitcast.563, f32[1,8192]{1,0:T(1,128)S(1)} %bitcast.562, f32[1,8192]{1,0:T(1,128)S(1)} %bitcast.561, f32[1,8192]{1,0:T(1,128)S(1)} %bitcast.450, f32[1,8192]{1,0:T(1,128)S(1)} %bitcast.451, f32[1,8192]{1,0:T(1,128)S(1)} %bitcast.452, f32[1,8192]{1,0:T(1,128)} %bitcast.611, f32[1,8192]{1,0:T(1,128)} %bitcast.607, ...), dimensions={0} | concatenate | bytes 1572864 | tf_op jit(solution)/shard_map/stack | solution.py:90
  79.0 3.4 %stack.29 = f32[24,8192]{1,0:T(8,128)S(1)} concatenate(f32[1,8192]{1,0:T(1,128)S(1)} %bitcast.549, f32[1,8192]{1,0:T(1,128)S(1)} %bitcast.548, f32[1,8192]{1,0:T(1,128)S(1)} %bitcast.547, f32[1,8192]{1,0:T(1,128)S(1)} %bitcast.438, f32[1,8192]{1,0:T(1,128)S(1)} %bitcast.439, f32[1,8192]{1,0:T(1,128)S(1)} %bitcast.440, f32[1,8192]{1,0:T(1,128)} %bitcast.602, f32[1,8192]{1,0:T(1,128)} %bitcast.601, ...), dimensions={0} | concatenate | bytes 1572864 | tf_op jit(solution)/shard_map/stack | solution.py:90
  86.8 8.2 %collective-permute-start.6 = (f32[2,8,128]{2,1,0:T(8,128)S(1)}, f32[2,8,128]{2,1,0:T(8,128)S(1)}, u32[]{:S(2)}, u32[]{:S(2)}) collective-permute-start(f32[2,8,128]{2,1,0:T(8,128)S(1)} %get-tuple-element.212), channel_id=1, source_target_pairs={{0,16},{16,32},{32,48},{48,64},{64,80},{80,96},{96,112},{112,128},... | collective-permute-start | bytes 24584 | tf_op jit(solution)/shard_map/ppermute | solution.py:22
  94.9 1.9 collective-permute-start.7
  96.9 6.9 %collective-permute-done.7 = f32[2,8,128]{2,1,0:T(8,128)S(1)} collective-permute-done((f32[2,8,128]{2,1,0:T(8,128)S(1)}, f32[2,8,128]{2,1,0:T(8,128)S(1)}, u32[]{:S(2)}, u32[]{:S(2)}) %collective-permute-start.7) | collective-permute-done | bytes 8224 | tf_op jit(solution)/shard_map/ppermute | solution.py:24
  103.8 3.1 %collective-permute-start.8 = (f32[12,2,128]{2,1,0:T(2,128)S(1)}, f32[12,2,128]{2,1,0:T(2,128)S(1)}, u32[]{:S(2)}, u32[]{:S(2)}) collective-permute-start(f32[12,2,128]{2,1,0:T(2,128)S(1)} %get-tuple-element.203), channel_id=1, source_target_pairs={{0,1},{1,2},{2,3},{3,4},{4,5},{5,6},{6,7},{7,8},{8,9},{9,10},{10,1... | collective-permute-start | bytes 36872 | tf_op jit(solution)/shard_map/ppermute | solution.py:22
  108.4 5.7 %collective-permute-done.9 = f32[12,2,128]{2,1,0:T(2,128)S(1)} collective-permute-done((f32[12,2,128]{2,1,0:T(2,128)S(1)}, f32[12,2,128]{2,1,0:T(2,128)S(1)}, u32[]{:S(2)}, u32[]{:S(2)}) %collective-permute-start.9) | collective-permute-done | bytes 12320 | tf_op jit(solution)/shard_map/ppermute | solution.py:24
  116.1 111.8 %psum.7 = f32[63,64]{1,0:T(8,128)S(1)} all-reduce(f32[63,64]{1,0:T(8,128)S(1)} %copy.118), channel_id=1, replica_groups=mesh['gx'=32,'gy'=16] {'gx','gy'}, use_global_device_ids=true, to_apply=%region_10.11 | all-reduce | flops 4032 | bytes 32256 | tf_op jit(solution)/shard_map/psum | solution.py:176
  (206 shorter events, 32.0 us)
Async XLA Ops:
  0.6 49.0 %copy-start = (f32[24,24]{1,0:T(8,128)S(1)}, f32[24,24]{1,0:T(8,128)}, u32[]{:S(2)}) copy-start(f32[24,24]{1,0:T(8,128)} %param.14) | copy-start | bytes 6916
  0.6 17.0 %copy-start.3 = (f32[8,8,128]{2,1,0:T(8,128)S(1)}, f32[8,8,128]{2,1,0:T(8,128)}, u32[]{:S(2)}) copy-start(f32[8,8,128]{2,1,0:T(8,128)} %param.9) | copy-start | bytes 98308
  1.4 16.8 %collective-permute-start.1 = (f32[2,8,128]{2,1,0:T(8,128)S(1)}, f32[2,8,128]{2,1,0:T(8,128)S(1)}, u32[]{:S(2)}, u32[]{:S(2)}) collective-permute-start(f32[2,8,128]{2,1,0:T(8,128)S(1)} %get-tuple-element.214), channel_id=1, source_target_pairs={{16,0},{32,16},{48,32},{64,48},{80,64},{96,80},{112,96},{128,112},... | collective-permute-start | bytes 24584 | tf_op jit(solution)/shard_map/ppermute | solution.py:24
  10.2 7.4 %collective-permute-start = (f32[2,8,128]{2,1,0:T(8,128)S(1)}, f32[2,8,128]{2,1,0:T(8,128)S(1)}, u32[]{:S(2)}, u32[]{:S(2)}) collective-permute-start(f32[2,8,128]{2,1,0:T(8,128)S(1)} %get-tuple-element.215), channel_id=1, source_target_pairs={{0,16},{16,32},{32,48},{48,64},{64,80},{80,96},{96,112},{112,128},... | collective-permute-start | bytes 24584 | tf_op jit(solution)/shard_map/ppermute | solution.py:22
  14.2 11.1 %collective-permute-start.4 = (f32[4,2,3,1,8,128]{5,4,3,2,1,0:T(8,128)S(1)}, f32[4,2,3,1,8,128]{5,4,3,2,1,0:T(8,128)S(1)}, u32[]{:S(2)}, u32[]{:S(2)}) collective-permute-start(f32[4,2,3,1,8,128]{5,4,3,2,1,0:T(8,128)S(1)} %slice.2424), channel_id=1, source_target_pairs={{16,0},{32,16},{48,32},{64,48},{80,64},{96,80},{112,96},{128,112},... | collective-permute-start | bytes 294920 | tf_op jit(solution)/shard_map/ppermute | solution.py:34
  18.3 4.1 %collective-permute-start.2 = (f32[12,2,128]{2,1,0:T(2,128)S(1)}, f32[12,2,128]{2,1,0:T(2,128)S(1)}, u32[]{:S(2)}, u32[]{:S(2)}) collective-permute-start(f32[12,2,128]{2,1,0:T(2,128)S(1)} %get-tuple-element.205), channel_id=1, source_target_pairs={{0,1},{1,2},{2,3},{3,4},{4,5},{5,6},{6,7},{7,8},{8,9},{9,10},{10,1... | collective-permute-start | bytes 36872 | tf_op jit(solution)/shard_map/ppermute | solution.py:22
  20.6 4.6 %collective-permute-start.3 = (f32[12,2,128]{2,1,0:T(2,128)S(1)}, f32[12,2,128]{2,1,0:T(2,128)S(1)}, u32[]{:S(2)}, u32[]{:S(2)}) collective-permute-start(f32[12,2,128]{2,1,0:T(2,128)S(1)} %get-tuple-element.206), channel_id=1, source_target_pairs={{1,0},{2,1},{3,2},{4,3},{5,4},{6,5},{7,6},{8,7},{9,8},{10,9},{11,1... | collective-permute-start | bytes 36872 | tf_op jit(solution)/shard_map/ppermute | solution.py:24
  25.4 8.5 %collective-permute-start.5 = (f32[4,2,3,9,1,128]{5,3,4,2,1,0:T(8,128)S(1)}, f32[4,2,3,9,1,128]{5,3,4,2,1,0:T(8,128)S(1)}, u32[]{:S(2)}, u32[]{:S(2)}) collective-permute-start(f32[4,2,3,9,1,128]{5,3,4,2,1,0:T(8,128)S(1)} %copy.114), channel_id=1, source_target_pairs={{1,0},{2,1},{3,2},{4,3},{5,4},{6,5},{7,6},{8,7},{9,8},{10,9},{11,1... | collective-permute-start | bytes 331784 | tf_op jit(solution)/shard_map/ppermute | solution.py:34
  43.8 8.5 %copy-start.4 = (f32[24,24]{1,0:T(8,128)S(1)}, f32[24,24]{1,0:T(8,128)}, u32[]{:S(2)}) copy-start(f32[24,24]{1,0:T(8,128)} %param.13) | copy-start | bytes 6916
  68.3 4.8 %copy-start.12 = (f32[1,1,1,8,8,128]{5,4,3,2,1,0:T(8,128)S(1)}, f32[1,1,1,8,8,128]{5,4,3,2,1,0:T(8,128)}, u32[]{:S(2)}) copy-start(f32[1,1,1,8,8,128]{5,4,3,2,1,0:T(8,128)} %get-tuple-element.19) | copy-start | bytes 98308
  68.3 4.8 %copy-start.13 = (f32[1,1,1,8,8,128]{5,4,3,2,1,0:T(8,128)S(1)}, f32[1,1,1,8,8,128]{5,4,3,2,1,0:T(8,128)}, u32[]{:S(2)}) copy-start(f32[1,1,1,8,8,128]{5,4,3,2,1,0:T(8,128)} %get-tuple-element.20) | copy-start | bytes 98308
  68.4 4.8 %copy-start.14 = (f32[1,1,1,8,8,128]{5,4,3,2,1,0:T(8,128)S(1)}, f32[1,1,1,8,8,128]{5,4,3,2,1,0:T(8,128)}, u32[]{:S(2)}) copy-start(f32[1,1,1,8,8,128]{5,4,3,2,1,0:T(8,128)} %get-tuple-element.21) | copy-start | bytes 98308
  68.4 4.8 %copy-start.15 = (f32[1,1,1,8,8,128]{5,4,3,2,1,0:T(8,128)S(1)}, f32[1,1,1,8,8,128]{5,4,3,2,1,0:T(8,128)}, u32[]{:S(2)}) copy-start(f32[1,1,1,8,8,128]{5,4,3,2,1,0:T(8,128)} %get-tuple-element.22) | copy-start | bytes 98308
  68.4 4.8 %copy-start.16 = (f32[1,1,1,8,8,128]{5,4,3,2,1,0:T(8,128)S(1)}, f32[1,1,1,8,8,128]{5,4,3,2,1,0:T(8,128)}, u32[]{:S(2)}) copy-start(f32[1,1,1,8,8,128]{5,4,3,2,1,0:T(8,128)} %get-tuple-element.23) | copy-start | bytes 98308
  85.5 11.4 %copy-start.60 = (s32[1,64,1]{1,2,0:T(1,128)S(1)}, s32[1,64,1]{1,2,0:T(1,128)}, u32[]{:S(2)}) copy-start(s32[1,64,1]{1,2,0:T(1,128)} %broadcast_bitcast_fusion) | copy-start | bytes 772
  85.5 22.7 %copy-start.56 = (f32[63,64]{0,1:T(8,128)S(1)}, f32[63,64]{0,1:T(8,128)}, u32[]{:S(2)}) copy-start(f32[63,64]{0,1:T(8,128)} %constant.25.clone.1) | copy-start | bytes 48388
  86.8 10.1 %collective-permute-start.6 = (f32[2,8,128]{2,1,0:T(8,128)S(1)}, f32[2,8,128]{2,1,0:T(8,128)S(1)}, u32[]{:S(2)}, u32[]{:S(2)}) collective-permute-start(f32[2,8,128]{2,1,0:T(8,128)S(1)} %get-tuple-element.212), channel_id=1, source_target_pairs={{0,16},{16,32},{32,48},{48,64},{64,80},{80,96},{96,112},{112,128},... | collective-permute-start | bytes 24584 | tf_op jit(solution)/shard_map/ppermute | solution.py:22
  94.9 8.9 %collective-permute-start.7 = (f32[2,8,128]{2,1,0:T(8,128)S(1)}, f32[2,8,128]{2,1,0:T(8,128)S(1)}, u32[]{:S(2)}, u32[]{:S(2)}) collective-permute-start(f32[2,8,128]{2,1,0:T(8,128)S(1)} %get-tuple-element.213), channel_id=1, source_target_pairs={{16,0},{32,16},{48,32},{64,48},{80,64},{96,80},{112,96},{128,112},... | collective-permute-start | bytes 24584 | tf_op jit(solution)/shard_map/ppermute | solution.py:24
  103.8 4.6 %collective-permute-start.8 = (f32[12,2,128]{2,1,0:T(2,128)S(1)}, f32[12,2,128]{2,1,0:T(2,128)S(1)}, u32[]{:S(2)}, u32[]{:S(2)}) collective-permute-start(f32[12,2,128]{2,1,0:T(2,128)S(1)} %get-tuple-element.203), channel_id=1, source_target_pairs={{0,1},{1,2},{2,3},{3,4},{4,5},{5,6},{6,7},{7,8},{8,9},{9,10},{10,1... | collective-permute-start | bytes 36872 | tf_op jit(solution)/shard_map/ppermute | solution.py:22
  106.9 7.1 %collective-permute-start.9 = (f32[12,2,128]{2,1,0:T(2,128)S(1)}, f32[12,2,128]{2,1,0:T(2,128)S(1)}, u32[]{:S(2)}, u32[]{:S(2)}) collective-permute-start(f32[12,2,128]{2,1,0:T(2,128)S(1)} %get-tuple-element.204), channel_id=1, source_target_pairs={{1,0},{2,1},{3,2},{4,3},{5,4},{6,5},{7,6},{8,7},{9,8},{10,9},{11,1... | collective-permute-start | bytes 36872 | tf_op jit(solution)/shard_map/ppermute | solution.py:24
  108.4 6.5 %copy-start.57 = (f32[8,8,128]{2,1,0:T(8,128)S(1)}, f32[8,8,128]{2,1,0:T(8,128)}, u32[]{:S(2)}) copy-start(f32[8,8,128]{2,1,0:T(8,128)} %get-tuple-element.207) | copy-start | bytes 98308
  108.4 6.5 %copy-start.58 = (f32[8,8,128]{2,1,0:T(8,128)S(1)}, f32[8,8,128]{2,1,0:T(8,128)}, u32[]{:S(2)}) copy-start(f32[8,8,128]{2,1,0:T(8,128)} %get-tuple-element.208) | copy-start | bytes 98308
  114.3 114.4 %copy-start.59 = (f32[64]{0:T(128)S(1)}, f32[64]{0:T(128)}, u32[]{:S(2)}) copy-start(f32[64]{0:T(128)} %param.15) | copy-start | bytes 772
  114.8 118.4 %copy-start.30 = (f32[8,8,128]{2,1,0:T(8,128)}, f32[8,8,128]{2,1,0:T(8,128)S(1)}, u32[]{:S(2)}) copy-start(f32[8,8,128]{2,1,0:T(8,128)S(1)} %get-tuple-element.6) | copy-start | bytes 98308
  (47 other events, 149.3 us)
where the time goes:
time: 236 us; the launch traced here: 234 us
  blocking collectives  112 us (47%)
  local copies, waits for them, and re-layouts  46.5 us (20%)
  starting transfers between devices  32.5 us (14%)
  waiting for transfers between devices  20.3 us (9%)
  matrix products  11.7 us (5%)
  other arithmetic  9.3 us (4%)
    psum x1, blocking collectives, bisect_round(): volumes = lax.psum(partial_volumes, ('gx', 'gy'))  112 us
    another operation x8, local copies, waits for them, and re-layouts, element_terms(): vectors.append(jnp.stack(row_list))  31 us
    ppermute x4, starting transfers between devices, with_halo(): lax.ppermute(tail, axis, [(i, (i + 1) % count) for i in range(ends)])  15.6 us
    ppermute x4, waiting for transfers between devices, with_halo(): lax.ppermute(head, axis, [((i + 1) % count, i) for i in range(ends)])  15.3 us
    ppermute x4, starting transfers between devices, with_halo(): lax.ppermute(head, axis, [((i + 1) % count, i) for i in range(ends)])  13.3 us
    slice x9, local copies, waits for them, and re-layouts, element_terms(): extended[pair_index, member, component, corner_x:corner_x + cells_x, corn...  8.41 us
    dot_general x4, matrix products, element_terms(): jnp.dot(mass_matrix, adjoint_rows, precision=lax.Precision.HIGHEST)  7.02 us
    ppermute x2, waiting for transfers between devices, from_behind(): lax.ppermute(value, axis, [(source, source + steps) for source in range(i...  4.95 us
  transfers between devices with their start and end apart: 10, of which 4 were waited for; matrix products, arithmetic and copies ran while one was open for 3% of the time, Pallas kernels for 0%

commit v1 on v0

--- a/solution.py
+++ b/solution.py
@@ -3,6 +3,7 @@
 import jax.numpy as jnp
 from jax import lax
 from jax.sharding import PartitionSpec as P
+from jax.lax import psum
 
 BISECT = 6
 REGIONS = 64
@@ -173,7 +174,13 @@
         partial_volumes = (
             jnp.sum(fields_of, axis=(1, 2)).reshape(len(midpoints), REGIONS, band_cells).sum(axis=2)
         )
-        volumes = lax.psum(partial_volumes, ("gx", "gy"))
+
+        def part_target(array_in):
+            for u in ("gx", "gy"):
+                array_in = psum(array_in, u)
+            return array_in
+
+        volumes = part_target(partial_volumes)
         position = jnp.zeros((REGIONS,), jnp.int32)
         for depth in range(levels):
             middle = jnp.sqrt(low_end * high_end)

time: 236 us -> 379 us (1.61)
  the two profiles are of different devices: /device:TPU:1 before, /device:TPU:256 now
where the time goes in v1:
time: 379 us; the launch traced here: 377 us
  blocking collectives  253 us (67%)
  local copies, waits for them, and re-layouts  46.4 us (12%)
  starting transfers between devices  38.7 us (10%)
  waiting for transfers between devices  16.2 us (4%)
  matrix products  11.6 us (3%)
  other arithmetic  9.26 us (2%)
    psum x2, blocking collectives, part_target(): array_in = psum(array_in, u)  253 us
    another operation x8, local copies, waits for them, and re-layouts, element_terms(): vectors.append(jnp.stack(row_list))  30.8 us
    ppermute x4, starting transfers between devices, with_halo(): lax.ppermute(head, axis, [((i + 1) % count, i) for i in range(ends)])  18.5 us
    ppermute x4, waiting for transfers between devices, with_halo(): lax.ppermute(head, axis, [((i + 1) % count, i) for i in range(ends)])  12.2 us
    ppermute x2, starting transfers between devices, from_behind(): lax.ppermute(value, axis, [(source, source + steps) for source in range(i...  11 us
    ppermute x4, starting transfers between devices, with_halo(): lax.ppermute(tail, axis, [(i, (i + 1) % count) for i in range(ends)])  9.22 us
    slice x9, local copies, waits for them, and re-layouts, element_terms(): extended[pair_index, member, component, corner_x:corner_x + cells_x, corn...  8.3 us
  transfers between devices with their start and end apart: 10, of which 4 were waited for; matrix products, arithmetic and copies ran while one was open for 2% of the time, Pallas kernels for 0%

profile of v1, /device:TPU:256, one launch (start us, length us, event | category | flops | bytes accessed | tf_op | source)
XLA Modules:
  0.0 376.7 jit_solution(18373509777490403360)
XLA Ops:
  1.4 6.3 %collective-permute-start.1 = (f32[2,8,128]{2,1,0:T(8,128)S(1)}, f32[2,8,128]{2,1,0:T(8,128)S(1)}, u32[]{:S(2)}, u32[]{:S(2)}) collective-permute-start(f32[2,8,128]{2,1,0:T(8,128)S(1)} %get-tuple-element.214), channel_id=1, source_target_pairs={{16,0},{32,16},{48,32},{64,48},{80,64},{96,80},{112,96},{128,112},... | collective-permute-start | bytes 24584 | tf_op jit(solution)/shard_map/ppermute | solution.py:25
  7.7 1.9 collective-permute-start
  11.6 9.7 %collective-permute-start.4 = (f32[4,2,3,1,8,128]{5,4,3,2,1,0:T(8,128)S(1)}, f32[4,2,3,1,8,128]{5,4,3,2,1,0:T(8,128)S(1)}, u32[]{:S(2)}, u32[]{:S(2)}) collective-permute-start(f32[4,2,3,1,8,128]{5,4,3,2,1,0:T(8,128)S(1)} %slice.2424), channel_id=1, source_target_pairs={{16,0},{32,16},{48,32},{64,48},{80,64},{96,80},{112,96},{128,112},... | collective-permute-start | bytes 294920 | tf_op jit(solution)/shard_map/ppermute | solution.py:35
  23.0 2.6 collective-permute-start.2
  27.5 4.0 %collective-permute-done.3 = f32[12,2,128]{2,1,0:T(2,128)S(1)} collective-permute-done((f32[12,2,128]{2,1,0:T(2,128)S(1)}, f32[12,2,128]{2,1,0:T(2,128)S(1)}, u32[]{:S(2)}, u32[]{:S(2)}) %collective-permute-start.3) | collective-permute-done | bytes 12320 | tf_op jit(solution)/shard_map/ppermute | solution.py:25
  35.3 4.0 %collective-permute-done.5 = f32[4,2,3,9,1,128]{5,3,4,2,1,0:T(8,128)S(1)} collective-permute-done((f32[4,2,3,9,1,128]{5,3,4,2,1,0:T(8,128)S(1)}, f32[4,2,3,9,1,128]{5,3,4,2,1,0:T(8,128)S(1)}, u32[]{:S(2)}, u32[]{:S(2)}) %collective-permute-start.5) | collective-permute-done | bytes 110624 | tf_op jit(solution)/shard_map/ppermute | solution.py:35
  45.3 3.7 stack.24
  49.0 5.8 %stack.25 = f32[24,8192]{1,0:T(8,128)} concatenate(f32[1,8192]{1,0:T(1,128)} %bitcast.571, f32[1,8192]{1,0:T(1,128)} %bitcast.570, f32[1,8192]{1,0:T(1,128)} %bitcast.588, f32[1,8192]{1,0:T(1,128)} %bitcast.468, f32[1,8192]{1,0:T(1,128)} %bitcast.469, f32[1,8192]{1,0:T(1,128)} %bitcast.470, f32[1,8192]{1,0:T(1,128)} %bitcast.617, f32[1,8192]{1,0:T(1,128)} %bitcast.616, ...), dimensions={0} | concatenate | bytes 1572864 | tf_op jit(solution)/shard_map/stack | solution.py:91
  54.8 2.7 fusion.17
  57.4 1.5 fusion.13
  58.9 3.7 stack.31
  62.6 5.8 %stack.30 = f32[24,8192]{1,0:T(8,128)} concatenate(f32[1,8192]{1,0:T(1,128)} %bitcast.558, f32[1,8192]{1,0:T(1,128)} %bitcast.557, f32[1,8192]{1,0:T(1,128)} %bitcast.556, f32[1,8192]{1,0:T(1,128)} %bitcast.466, f32[1,8192]{1,0:T(1,128)} %bitcast.479, f32[1,8192]{1,0:T(1,128)} %bitcast.480, f32[1,8192]{1,0:T(1,128)} %bitcast.513, f32[1,8192]{1,0:T(1,128)} %bitcast.512, ...), dimensions={0} | concatenate | bytes 1572864 | tf_op jit(solution)/shard_map/stack | solution.py:91
  68.4 2.7 fusion.20
  71.0 1.5 fusion.16
  74.5 3.6 stack.27
  78.4 3.6 stack.26
  84.1 3.4 stack.29
  91.9 1.9 collective-permute-start.6
  93.8 9.7 %collective-permute-start.7 = (f32[2,8,128]{2,1,0:T(8,128)S(1)}, f32[2,8,128]{2,1,0:T(8,128)S(1)}, u32[]{:S(2)}, u32[]{:S(2)}) collective-permute-start(f32[2,8,128]{2,1,0:T(8,128)S(1)} %get-tuple-element.213), channel_id=1, source_target_pairs={{16,0},{32,16},{48,32},{64,48},{80,64},{96,80},{112,96},{128,112},... | collective-permute-start | bytes 24584 | tf_op jit(solution)/shard_map/ppermute | solution.py:25
  103.5 1.3 collective-permute-done.7
  104.8 2.8 collective-permute-start.8
  109.1 6.9 %collective-permute-done.9 = f32[12,2,128]{2,1,0:T(2,128)S(1)} collective-permute-done((f32[12,2,128]{2,1,0:T(2,128)S(1)}, f32[12,2,128]{2,1,0:T(2,128)S(1)}, u32[]{:S(2)}, u32[]{:S(2)}) %collective-permute-start.9) | collective-permute-done | bytes 12320 | tf_op jit(solution)/shard_map/ppermute | solution.py:25
  118.0 173.5 %psum.14 = f32[63,64]{1,0:T(8,128)S(1)} all-reduce(f32[63,64]{1,0:T(8,128)S(1)} %copy.118), channel_id=1, replica_groups=mesh['gx'=32,'gy'=16] {'gx'}, use_global_device_ids=true, to_apply=%region_10.11 | all-reduce | flops 4032 | bytes 32256 | tf_op jit(solution)/shard_map/psum | solution.py:180
  291.5 79.2 %psum.15 = f32[63,64]{1,0:T(8,128)S(1)} all-reduce(f32[63,64]{1,0:T(8,128)S(1)} %psum.14), channel_id=1, replica_groups=mesh['gx'=32,'gy'=16] {'gy'}, use_global_device_ids=true, to_apply=%region_11.12 | all-reduce | flops 4032 | bytes 32256 | tf_op jit(solution)/shard_map/psum | solution.py:180
  (207 shorter events, 33.2 us)
Async XLA Ops:
  0.6 54.1 %copy-start = (f32[24,24]{1,0:T(8,128)S(1)}, f32[24,24]{1,0:T(8,128)}, u32[]{:S(2)}) copy-start(f32[24,24]{1,0:T(8,128)} %param.14) | copy-start | bytes 6916
  0.6 21.7 %copy-start.3 = (f32[8,8,128]{2,1,0:T(8,128)S(1)}, f32[8,8,128]{2,1,0:T(8,128)}, u32[]{:S(2)}) copy-start(f32[8,8,128]{2,1,0:T(8,128)} %param.9) | copy-start | bytes 98308
  1.4 21.5 %collective-permute-start.1 = (f32[2,8,128]{2,1,0:T(8,128)S(1)}, f32[2,8,128]{2,1,0:T(8,128)S(1)}, u32[]{:S(2)}, u32[]{:S(2)}) collective-permute-start(f32[2,8,128]{2,1,0:T(8,128)S(1)} %get-tuple-element.214), channel_id=1, source_target_pairs={{16,0},{32,16},{48,32},{64,48},{80,64},{96,80},{112,96},{128,112},... | collective-permute-start | bytes 24584 | tf_op jit(solution)/shard_map/ppermute | solution.py:25
  7.7 14.6 %collective-permute-start = (f32[2,8,128]{2,1,0:T(8,128)S(1)}, f32[2,8,128]{2,1,0:T(8,128)S(1)}, u32[]{:S(2)}, u32[]{:S(2)}) collective-permute-start(f32[2,8,128]{2,1,0:T(8,128)S(1)} %get-tuple-element.215), channel_id=1, source_target_pairs={{0,16},{16,32},{32,48},{48,64},{64,80},{80,96},{96,112},{112,128},... | collective-permute-start | bytes 24584 | tf_op jit(solution)/shard_map/ppermute | solution.py:23
  11.6 20.0 %collective-permute-start.4 = (f32[4,2,3,1,8,128]{5,4,3,2,1,0:T(8,128)S(1)}, f32[4,2,3,1,8,128]{5,4,3,2,1,0:T(8,128)S(1)}, u32[]{:S(2)}, u32[]{:S(2)}) collective-permute-start(f32[4,2,3,1,8,128]{5,4,3,2,1,0:T(8,128)S(1)} %slice.2424), channel_id=1, source_target_pairs={{16,0},{32,16},{48,32},{64,48},{80,64},{96,80},{112,96},{128,112},... | collective-permute-start | bytes 294920 | tf_op jit(solution)/shard_map/ppermute | solution.py:35
  23.0 4.5 %collective-permute-start.2 = (f32[12,2,128]{2,1,0:T(2,128)S(1)}, f32[12,2,128]{2,1,0:T(2,128)S(1)}, u32[]{:S(2)}, u32[]{:S(2)}) collective-permute-start(f32[12,2,128]{2,1,0:T(2,128)S(1)} %get-tuple-element.205), channel_id=1, source_target_pairs={{0,1},{1,2},{2,3},{3,4},{4,5},{5,6},{6,7},{7,8},{8,9},{9,10},{10,1... | collective-permute-start | bytes 36872 | tf_op jit(solution)/shard_map/ppermute | solution.py:23
  25.6 5.9 %collective-permute-start.3 = (f32[12,2,128]{2,1,0:T(2,128)S(1)}, f32[12,2,128]{2,1,0:T(2,128)S(1)}, u32[]{:S(2)}, u32[]{:S(2)}) collective-permute-start(f32[12,2,128]{2,1,0:T(2,128)S(1)} %get-tuple-element.206), channel_id=1, source_target_pairs={{1,0},{2,1},{3,2},{4,3},{5,4},{6,5},{7,6},{8,7},{9,8},{10,9},{11,1... | collective-permute-start | bytes 36872 | tf_op jit(solution)/shard_map/ppermute | solution.py:25
  31.7 7.6 %collective-permute-start.5 = (f32[4,2,3,9,1,128]{5,3,4,2,1,0:T(8,128)S(1)}, f32[4,2,3,9,1,128]{5,3,4,2,1,0:T(8,128)S(1)}, u32[]{:S(2)}, u32[]{:S(2)}) collective-permute-start(f32[4,2,3,9,1,128]{5,3,4,2,1,0:T(8,128)S(1)} %copy.114), channel_id=1, source_target_pairs={{1,0},{2,1},{3,2},{4,3},{5,4},{6,5},{7,6},{8,7},{9,8},{10,9},{11,1... | collective-permute-start | bytes 331784 | tf_op jit(solution)/shard_map/ppermute | solution.py:35
  49.0 8.4 %copy-start.4 = (f32[24,24]{1,0:T(8,128)S(1)}, f32[24,24]{1,0:T(8,128)}, u32[]{:S(2)}) copy-start(f32[24,24]{1,0:T(8,128)} %param.13) | copy-start | bytes 6916
  73.4 4.8 %copy-start.12 = (f32[1,1,1,8,8,128]{5,4,3,2,1,0:T(8,128)S(1)}, f32[1,1,1,8,8,128]{5,4,3,2,1,0:T(8,128)}, u32[]{:S(2)}) copy-start(f32[1,1,1,8,8,128]{5,4,3,2,1,0:T(8,128)} %get-tuple-element.19) | copy-start | bytes 98308
  73.4 4.8 %copy-start.13 = (f32[1,1,1,8,8,128]{5,4,3,2,1,0:T(8,128)S(1)}, f32[1,1,1,8,8,128]{5,4,3,2,1,0:T(8,128)}, u32[]{:S(2)}) copy-start(f32[1,1,1,8,8,128]{5,4,3,2,1,0:T(8,128)} %get-tuple-element.20) | copy-start | bytes 98308
  73.4 4.8 %copy-start.14 = (f32[1,1,1,8,8,128]{5,4,3,2,1,0:T(8,128)S(1)}, f32[1,1,1,8,8,128]{5,4,3,2,1,0:T(8,128)}, u32[]{:S(2)}) copy-start(f32[1,1,1,8,8,128]{5,4,3,2,1,0:T(8,128)} %get-tuple-element.21) | copy-start | bytes 98308
  73.5 4.8 %copy-start.15 = (f32[1,1,1,8,8,128]{5,4,3,2,1,0:T(8,128)S(1)}, f32[1,1,1,8,8,128]{5,4,3,2,1,0:T(8,128)}, u32[]{:S(2)}) copy-start(f32[1,1,1,8,8,128]{5,4,3,2,1,0:T(8,128)} %get-tuple-element.22) | copy-start | bytes 98308
  73.5 4.8 %copy-start.16 = (f32[1,1,1,8,8,128]{5,4,3,2,1,0:T(8,128)S(1)}, f32[1,1,1,8,8,128]{5,4,3,2,1,0:T(8,128)}, u32[]{:S(2)}) copy-start(f32[1,1,1,8,8,128]{5,4,3,2,1,0:T(8,128)} %get-tuple-element.23) | copy-start | bytes 98308
  90.6 12.9 %copy-start.60 = (s32[1,64,1]{1,2,0:T(1,128)S(1)}, s32[1,64,1]{1,2,0:T(1,128)}, u32[]{:S(2)}) copy-start(s32[1,64,1]{1,2,0:T(1,128)} %broadcast_bitcast_fusion) | copy-start | bytes 772
  90.6 18.3 %copy-start.56 = (f32[63,64]{0,1:T(8,128)S(1)}, f32[63,64]{0,1:T(8,128)}, u32[]{:S(2)}) copy-start(f32[63,64]{0,1:T(8,128)} %constant.25.clone.1) | copy-start | bytes 48388
  91.9 11.6 %collective-permute-start.6 = (f32[2,8,128]{2,1,0:T(8,128)S(1)}, f32[2,8,128]{2,1,0:T(8,128)S(1)}, u32[]{:S(2)}, u32[]{:S(2)}) collective-permute-start(f32[2,8,128]{2,1,0:T(8,128)S(1)} %get-tuple-element.212), channel_id=1, source_target_pairs={{0,16},{16,32},{32,48},{48,64},{64,80},{80,96},{96,112},{112,128},... | collective-permute-start | bytes 24584 | tf_op jit(solution)/shard_map/ppermute | solution.py:23
  93.8 11.0 %collective-permute-start.7 = (f32[2,8,128]{2,1,0:T(8,128)S(1)}, f32[2,8,128]{2,1,0:T(8,128)S(1)}, u32[]{:S(2)}, u32[]{:S(2)}) collective-permute-start(f32[2,8,128]{2,1,0:T(8,128)S(1)} %get-tuple-element.213), channel_id=1, source_target_pairs={{16,0},{32,16},{48,32},{64,48},{80,64},{96,80},{112,96},{128,112},... | collective-permute-start | bytes 24584 | tf_op jit(solution)/shard_map/ppermute | solution.py:25
  104.8 4.3 %collective-permute-start.8 = (f32[12,2,128]{2,1,0:T(2,128)S(1)}, f32[12,2,128]{2,1,0:T(2,128)S(1)}, u32[]{:S(2)}, u32[]{:S(2)}) collective-permute-start(f32[12,2,128]{2,1,0:T(2,128)S(1)} %get-tuple-element.203), channel_id=1, source_target_pairs={{0,1},{1,2},{2,3},{3,4},{4,5},{5,6},{6,7},{7,8},{8,9},{9,10},{10,1... | collective-permute-start | bytes 36872 | tf_op jit(solution)/shard_map/ppermute | solution.py:23
  107.6 8.4 %collective-permute-start.9 = (f32[12,2,128]{2,1,0:T(2,128)S(1)}, f32[12,2,128]{2,1,0:T(2,128)S(1)}, u32[]{:S(2)}, u32[]{:S(2)}) collective-permute-start(f32[12,2,128]{2,1,0:T(2,128)S(1)} %get-tuple-element.204), channel_id=1, source_target_pairs={{1,0},{2,1},{3,2},{4,3},{5,4},{6,5},{7,6},{8,7},{9,8},{10,9},{11,1... | collective-permute-start | bytes 36872 | tf_op jit(solution)/shard_map/ppermute | solution.py:25
  109.1 7.7 %copy-start.57 = (f32[8,8,128]{2,1,0:T(8,128)S(1)}, f32[8,8,128]{2,1,0:T(8,128)}, u32[]{:S(2)}) copy-start(f32[8,8,128]{2,1,0:T(8,128)} %get-tuple-element.207) | copy-start | bytes 98308
  109.1 7.7 %copy-start.58 = (f32[8,8,128]{2,1,0:T(8,128)S(1)}, f32[8,8,128]{2,1,0:T(8,128)}, u32[]{:S(2)}) copy-start(f32[8,8,128]{2,1,0:T(8,128)} %get-tuple-element.208) | copy-start | bytes 98308
  116.2 255.3 %copy-start.59 = (f32[64]{0:T(128)S(1)}, f32[64]{0:T(128)}, u32[]{:S(2)}) copy-start(f32[64]{0:T(128)} %param.15) | copy-start | bytes 772
  116.8 259.3 %copy-start.30 = (f32[8,8,128]{2,1,0:T(8,128)}, f32[8,8,128]{2,1,0:T(8,128)S(1)}, u32[]{:S(2)}) copy-start(f32[8,8,128]{2,1,0:T(8,128)S(1)} %get-tuple-element.6) | copy-start | bytes 98308
  (47 other events, 149.4 us)
